TPU v7x, 256 devices: a whole 4x4x8 slice. The times are simulated.
256 devices in a mesh: dp: 64 (over x, z, core), tensor: 4 (over y).
Axes of the slice: x: 4, y: 4, z: 8, core: 2. Of those that a mesh axis runs over, the one named last changes fastest.
Arguments:
- tokens: bfloat16 [512, 16384], P('dp', 'tensor'), may hold values from -6 to 6
- clip_act: float32 [16384], P('tensor'), may hold values from 0.5 to 4
- weight: bfloat16 [16384, 49152], P('tensor', 'dp'), may hold values from -0.046875 to 0.046875
- clip_weight: float32 [49152], P('dp'), may hold values from 0.003 to 0.03
- cotangent: bfloat16 [512, 49152], P('tensor', 'dp'), may hold values from -16 to 16
Outputs:
- projected: bfloat16 [512, 49152], P('tensor', 'dp')
- token_grad: bfloat16 [512, 16384], P('dp', 'tensor')
- weight_grad: bfloat16 [16384, 49152], P('tensor', 'dp')
- clip_act_grad: float32 [16384], P('tensor')
- clip_weight_grad: float32 [49152], P('dp')
All inputs are finite; a program needn't handle non-finite values.
Results may differ from a plain program's by a relative error of at most 0.009.
Values may be sent and summed in bfloat16 or wider, within the bound.
No kernel may reach another device: no remote copies, remote signals or barrier semaphores. Data moves between devices by JAX's collectives and lax.ppermute only.
A program may use at most 128 MiB of HBM per device.

v0:
```python
import math
import jax
import jax.numpy as jnp
from jax import lax
from jax.sharding import PartitionSpec as P


def swapped(block, axis, bit):
    count = lax.axis_size(axis)
    route = []
    for low in range(count):
        high = low | 1 << bit
        if high != low and high < count:
            route += [(low, high), (high, low)]
    return lax.ppermute(block, axis, route)


def sylvester(order):
    index = lax.iota(jnp.int32, order)
    joined = jnp.bitwise_and(index[:, None], index[None, :])
    parity = jnp.zeros((order, order), jnp.int32)
    for bit_number in range(max(order.bit_length() - 1, 0)):
        parity = parity + jnp.bitwise_and(jnp.right_shift(joined, bit_number), 1)
    return (1 - 2 * jnp.bitwise_and(parity, 1)).astype(jnp.float32)


def local_rotate(values, norm_factor):
    row_total, width = values.shape
    levels = width.bit_length() - 1
    outer = 2 ** (levels // 2)
    inner = width // outer
    blocks = values.reshape(row_total, outer, inner)
    blocks = jnp.einsum("rab,ac->rcb", blocks, sylvester(outer), precision=lax.Precision.HIGHEST)
    blocks = jnp.einsum("rcb,bd->rcd", blocks, sylvester(inner), precision=lax.Precision.HIGHEST)
    return blocks.reshape(row_total, width) * norm_factor


def rotate(values):
    group_size = lax.axis_size("tensor")
    norm_factor = 1.0 / math.sqrt(values.shape[1] * group_size)
    mixed = local_rotate(values, norm_factor)
    position = lax.axis_index("tensor")
    for bit_number in range(group_size.bit_length() - 1):
        partner = swapped(mixed, "tensor", bit_number)
        upper = jnp.bitwise_and(jnp.right_shift(position, bit_number), 1) == 1
        mixed = jnp.where(upper, partner - mixed, mixed + partner)
    return mixed


def body(tokens, clip_act, weight, clip_weight, cotangent):
    rotated = rotate(tokens.astype(jnp.float32))
    ratio_act = rotated / clip_act
    tanh_act = jnp.tanh(ratio_act)
    quant_act = (clip_act * tanh_act).astype(jnp.bfloat16)
    slope_act = 1.0 - tanh_act * tanh_act
    edge_act = tanh_act - ratio_act * slope_act
    all_act = lax.all_gather(quant_act, "dp", axis=0, tiled=True)
    ratio_weight = weight.astype(jnp.float32) / clip_weight
    tanh_weight = jnp.tanh(ratio_weight)
    quant_weight = (clip_weight * tanh_weight).astype(jnp.bfloat16)
    block = all_act
    projected = lax.psum_scatter(
        jnp.dot(block, quant_weight, preferred_element_type=jnp.float32),
        "tensor",
        scatter_dimension=0,
        tiled=True,
    ).astype(jnp.bfloat16)
    all_cot = lax.all_gather(cotangent, "tensor", axis=0, tiled=True)
    weight_prod = lax.dot_general(
        all_act, all_cot, (((0,), (0,)), ((), ())), preferred_element_type=jnp.float32
    )
    slope_weight = 1.0 - tanh_weight * tanh_weight
    weight_grad = (weight_prod * slope_weight).astype(jnp.bfloat16)
    weight_terms = jnp.sum(weight_prod * (tanh_weight - ratio_weight * slope_weight), axis=0)
    clip_weight_grad = lax.psum(weight_terms, "tensor")
    block = all_cot
    act_prod = lax.psum_scatter(
        lax.dot_general(
            block, quant_weight, (((1,), (1,)), ((), ())), preferred_element_type=jnp.float32
        ),
        "dp",
        scatter_dimension=0,
        tiled=True,
    )
    clip_act_grad = lax.psum(jnp.sum(act_prod * edge_act, axis=0), "dp")
    pre_rotation = act_prod * slope_act
    token_grad = rotate(pre_rotation).astype(jnp.bfloat16)
    return (projected, token_grad, weight_grad, clip_act_grad, clip_weight_grad)


def solution(mesh):
    in_specs = (P("dp", "tensor"), P("tensor"), P("tensor", "dp"), P("dp"), P("tensor", "dp"))
    out_specs = (P("tensor", "dp"), P("dp", "tensor"), P("tensor", "dp"), P("tensor"), P("dp"))
    return jax.shard_map(body, mesh=mesh, in_specs=in_specs, out_specs=out_specs, check_vma=False)
```

profile of v0, /device:TPU:8, one launch (start us, length us, event | category | flops | bytes accessed | tf_op | source)
XLA Modules:
  0.0 489.3 jit_solution(6198169342169980642)
XLA Ops:
  7.2 14.6 %all_gather.7 = bf16[512,768]{1,0:T(8,128)(2,1)S(1)} all-gather(bf16[128,768]{1,0:T(8,128)(2,1)} %param.9), channel_id=1, replica_groups=mesh['dp'=64,'tensor'=4] {'tensor'}, dimensions={0}, use_global_device_ids=true | all-gather | bytes 983040 | tf_op jit(solution)/shard_map/all_gather | solution.py:68
  21.8 9.5 %convolution_bitcast_fusion = f32[512,4096]{0,1:T(8,128)} fusion(bf16[512,768]{1,0:T(8,128)(2,1)S(1)} %all_gather.7, f32[768]{0:T(1024)} %param.8, bf16[4096,768]{1,0:T(8,128)(2,1)} %param.7), kind=kOutput, calls=%fused_computation.5 | convolution fusion | flops 3233808384 | bytes 15469568 | tf_op jit(solution)/shard_map/dot_general | solution.py:78
  31.3 8.9 %copy.19 = f32[512,4096]{1,0:T(8,128)} copy(f32[512,4096]{0,1:T(8,128)} %convolution_bitcast_fusion) | data formatting | bytes 16777216
  40.3 0.8 copy-done
  41.1 0.2 reshape.24
  41.2 0.3 convolution_bitcast_fusion.2
  41.6 0.4 convolution_multiply_fusion.1
  42.1 2.0 collective-permute-start
  44.1 3.8 collective-permute-done
  47.9 2.7 collective-permute-start.1
  50.6 3.9 collective-permute-done.1
  54.5 140.9 %reduce-scatter.7.cloned.1.call-done = f32[8,4096]{1,0:T(8,128)} async-done(((f32[512,4096]{1,0:T(8,128)}), f32[8,4096]{1,0:T(8,128)}) %reduce-scatter.7.cloned.1.call-update) | async-done | bytes 131088 | tf_op jit(solution)/shard_map/reduce_scatter | solution.py:77
  195.4 1.0 multiply_reduce_fusion.1
  196.4 1.6 fusion
  198.1 0.4 convolution_bitcast_fusion.1
  198.5 0.4 convolution_multiply_fusion
  199.1 0.6 collective-permute-start.2
  199.7 246.6 %psum.14 = f32[4096]{0:T(1024)} all-reduce(f32[4096]{0:T(1024)S(1)} %get-tuple-element.10), channel_id=1, replica_groups=mesh['dp'=64,'tensor'=4] {'dp'}, use_global_device_ids=true, to_apply=%region_3.4 | all-reduce | flops 4096 | bytes 32768 | tf_op jit(solution)/shard_map/psum | solution.py:85
  446.2 2.6 collective-permute-start.3
  448.9 8.7 %fusion.33 = f32[512,768]{1,0:T(8,128)} fusion(bf16[512,4096]{1,0:T(8,128)(2,1)} %all-gather.2.cloned.1.call-done, f32[768]{0:T(1024)S(1)} %copy-done.2, bf16[4096,768]{1,0:T(8,128)(2,1)} %param.7), kind=kOutput, calls=%fused_computation.51 | convolution fusion | flops 3233808384 | bytes 12061696 | tf_op jit(solution)/shard_map/dot_general | solution.py:63
  457.6 0.7 select_convert_fusion
  458.3 12.4 %multiply_reduce_fusion = (f32[768]{0:T(1024)S(1)}, bf16[4096,768]{1,0:T(8,128)(2,1)}) fusion(f32[768]{0:T(1024)S(1)} %copy-done.2, bf16[4096,768]{1,0:T(8,128)(2,1)} %param.7, bf16[512,4096]{1,0:T(8,128)(2,1)} %all-gather.2.cloned.1.call-done, bf16[512,768]{1,0:T(8,128)(2,1)S(1)} %all_gather.7), kind=kOutput, calls=%fused_computation | convolution fusion | flops 3252681984 | bytes 17569792 | tf_op jit(solution)/shard_map/dot_general | solution.py:69
  470.7 10.4 %psum.15 = f32[768]{0:T(1024)} all-reduce(f32[768]{0:T(1024)S(1)} %get-tuple-element.12), channel_id=1, replica_groups=mesh['dp'=64,'tensor'=4] {'tensor'}, use_global_device_ids=true, to_apply=%region_5.6 | all-reduce | flops 768 | bytes 6144 | tf_op jit(solution)/shard_map/psum | solution.py:75
  481.1 1.7 convert_element_type.35
  (20 shorter events, 0.6 us)
Async XLA Ops:
  7.2 188.2 %reduce-scatter.7.cloned.1.call-start = ((), (), s32[]{:S(2)}) async-start(), calls=%async_computation.4 | async-start | bytes 8519680 | tf_op jit(solution)/shard_map/reduce_scatter | solution.py:77
  40.2 0.8 copy-start
  40.2 155.2 %copy-start.1 = (f32[4096]{0:T(1024)S(1)}, f32[4096]{0:T(1024)}, u32[]{:S(2)}) copy-start(f32[4096]{0:T(1024)} %param.6) | copy-start | bytes 49156
  40.2 408.7 %copy-start.2 = (f32[768]{0:T(1024)S(1)}, f32[768]{0:T(1024)}, u32[]{:S(2)}) copy-start(f32[768]{0:T(1024)} %param.8) | copy-start | bytes 9220
  40.2 408.6 %all-gather.2.cloned.1.call-start = ((), (), s32[]{:S(2)}) async-start(), calls=%async_computation.2 | async-start | bytes 4259840 | tf_op jit(solution)/shard_map/all_gather | solution.py:57
  42.1 5.8 %collective-permute-start = (f32[8,4096]{1,0:T(8,128)S(1)}, f32[8,4096]{1,0:T(8,128)S(1)}, u32[]{:S(2)}, u32[]{:S(2)}) collective-permute-start(f32[8,4096]{1,0:T(8,128)S(1)} %mul.67), channel_id=1, source_target_pairs={{0,1},{1,0},{2,3},{3,2},{4,5},{5,4},{6,7},{7,6},{8,9},{9,8},{10,11... | collective-permute-start | bytes 393224 | tf_op jit(solution)/shard_map/ppermute | solution.py:15
  47.9 6.6 %collective-permute-start.1 = (f32[8,4096]{1,0:T(8,128)S(1)}, f32[8,4096]{1,0:T(8,128)S(1)}, u32[]{:S(2)}, u32[]{:S(2)}) collective-permute-start(f32[8,4096]{1,0:T(8,128)S(1)} %add_select_fusion.1), channel_id=1, source_target_pairs={{0,2},{2,0},{1,3},{3,1},{4,6},{6,4},{5,7},{7,5},{8,10},{10,8},{9,1... | collective-permute-start | bytes 393224 | tf_op jit(solution)/shard_map/ppermute | solution.py:15
  198.0 283.1 %reduce-scatter.5.cloned.1.call-start = ((), (), s32[]{:S(2)}) async-start(), calls=%async_computation.3 | async-start | bytes 1966080 | tf_op jit(solution)/shard_map/reduce_scatter | solution.py:62
  199.1 247.2 %collective-permute-start.2 = (f32[8,4096]{1,0:T(8,128)S(1)}, f32[8,4096]{1,0:T(8,128)S(1)}, u32[]{:S(2)}, u32[]{:S(2)}) collective-permute-start(f32[8,4096]{1,0:T(8,128)S(1)} %mul.74), channel_id=1, source_target_pairs={{0,1},{1,0},{2,3},{3,2},{4,5},{5,4},{6,7},{7,6},{8,9},{9,8},{10,11... | collective-permute-start | bytes 393224 | tf_op jit(solution)/shard_map/ppermute | solution.py:15
  446.2 11.4 %collective-permute-start.3 = (f32[8,4096]{1,0:T(8,128)S(1)}, f32[8,4096]{1,0:T(8,128)S(1)}, u32[]{:S(2)}, u32[]{:S(2)}) collective-permute-start(f32[8,4096]{1,0:T(8,128)S(1)} %add_select_fusion), channel_id=1, source_target_pairs={{0,2},{2,0},{1,3},{3,1},{4,6},{6,4},{5,7},{7,5},{8,10},{10,8},{9,1... | collective-permute-start | bytes 393224 | tf_op jit(solution)/shard_map/ppermute | solution.py:15
Sparse Core Ops, SparseCore 0:
  40.4 154.9 reduce-scatter.6
  198.7 77.4 all-gather.1
  457.7 19.8 reduce-scatter.4
where the time goes:
time: 490 us; the launch traced here: 489 us
  blocking collectives  271 us (55%)
  waiting for transfers between devices  149 us (30%)
  matrix products  32.2 us (7%)
  between operations  13.8 us (3%)
  local copies, waits for them, and re-layouts  10.2 us (2%)
  starting transfers between devices  8.06 us (2%)
  other arithmetic  4.94 us (1%)
    psum x1, blocking collectives, body(): clip_act_grad = lax.psum(jnp.sum(act_prod * edge_act, axis=0), 'dp')  247 us
    reduce_scatter x1, waiting for transfers between devices, body(): lax.psum_scatter(lax.dot_general(block, quant_weight, (((1,), (1,)), ((),...  141 us
    all_gather x1, blocking collectives, body(): all_cot = lax.all_gather(cotangent, 'tensor', axis=0, tiled=True)  14.6 us
    dot_general x1, matrix products, body(): lax.dot_general(all_act, all_cot, (((0,), (0,)), ((), ())), preferred_ele...  12.4 us
    psum x1, blocking collectives, body(): clip_weight_grad = lax.psum(weight_terms, 'tensor')  10.4 us
  transfers between devices with their start and end apart: 7, of which 3 were waited for; matrix products, arithmetic and copies ran while one was open for 5% of the time, Pallas kernels for 0%

commit v1 on v0

--- a/solution.py
+++ b/solution.py
@@ -65,7 +65,9 @@
         scatter_dimension=0,
         tiled=True,
     ).astype(jnp.bfloat16)
-    all_cot = lax.all_gather(cotangent, "tensor", axis=0, tiled=True)
+    all_cot = jnp.concatenate(
+        lax.all_to_all(jnp.stack([cotangent] * lax.axis_size("tensor")), "tensor", 0, 0), axis=0
+    )
     weight_prod = lax.dot_general(
         all_act, all_cot, (((0,), (0,)), ((), ())), preferred_element_type=jnp.float32
     )

time: 490 us -> 491 us (level)
    all_to_all x0 -> x1, blocking collectives: none -> 15.5 us  [body(): lax.all_to_all(jnp.stack([cotangent] * lax.axis_size('tensor')), 'tensor'...]
    all_gather x1 -> x0, blocking collectives: 14.6 us -> none  [body(): all_cot = lax.all_gather(cotangent, 'tensor', axis=0, tiled=True)]
where the time goes in v1:
time: 491 us
  blocking collectives  272 us (55%)
  waiting for transfers between devices  149 us (30%)
  matrix products  32.2 us (7%)
  between operations  13.8 us (3%)
  local copies, waits for them, and re-layouts  11.2 us (2%)
  starting transfers between devices  6.52 us (1%)
  other arithmetic  4.94 us (1%)
    psum x1, blocking collectives, body(): clip_act_grad = lax.psum(jnp.sum(act_prod * edge_act, axis=0), 'dp')  247 us
    reduce_scatter x1, waiting for transfers between devices, body(): lax.psum_scatter(lax.dot_general(block, quant_weight, (((1,), (1,)), ((),...  141 us
    all_to_all x1, blocking collectives, body(): lax.all_to_all(jnp.stack([cotangent] * lax.axis_size('tensor')), 'tensor'...  15.5 us
    dot_general x1, matrix products, body(): lax.dot_general(all_act, all_cot, (((0,), (0,)), ((), ())), preferred_ele...  12.4 us
    psum x1, blocking collectives, body(): clip_weight_grad = lax.psum(weight_terms, 'tensor')  10.3 us
  transfers between devices with their start and end apart: 7, of which 3 were waited for; matrix products, arithmetic and copies ran while one was open for 5% of the time, Pallas kernels for 0%

profile of v1, /device:TPU:8, one launch (start us, length us, event | category | flops | bytes accessed | tf_op | source)
XLA Modules:
  0.0 490.5 jit_solution(15147431979704995441)
XLA Ops:
  7.2 1.0 stack.2
  8.2 15.5 %all_to_all.5 = bf16[4,128,768]{2,1,0:T(8,128)(2,1)S(1)} all-to-all(bf16[4,128,768]{2,1,0:T(8,128)(2,1)S(1)} %stack.2), channel_id=1, replica_groups=mesh['dp'=64,'tensor'=4] {'tensor'}, dimensions={0} | all-to-all | bytes 1572864 | tf_op jit(solution)/shard_map/all_to_all | solution.py:69
  23.7 9.5 %convolution_bitcast_fusion = f32[512,4096]{0,1:T(8,128)} fusion(bf16[512,768]{1,0:T(8,128)(2,1)S(1)} %bitcast.25, f32[768]{0:T(1024)} %param.8, bf16[4096,768]{1,0:T(8,128)(2,1)} %param.7), kind=kOutput, calls=%fused_computation.5 | convolution fusion | flops 3233808384 | bytes 15469568 | tf_op jit(solution)/shard_map/dot_general | solution.py:80
  33.2 8.9 %copy.19 = f32[512,4096]{1,0:T(8,128)} copy(f32[512,4096]{0,1:T(8,128)} %convolution_bitcast_fusion) | data formatting | bytes 16777216
  42.2 0.8 copy-done
  43.2 0.3 convolution_bitcast_fusion.2
  43.5 0.4 convolution_multiply_fusion.1
  44.0 1.5 collective-permute-start
  45.6 3.5 collective-permute-done
  49.1 1.6 collective-permute-start.1
  50.7 5.0 %collective-permute-done.1 = f32[8,4096]{1,0:T(8,128)S(1)} collective-permute-done((f32[8,4096]{1,0:T(8,128)S(1)}, f32[8,4096]{1,0:T(8,128)S(1)}, u32[]{:S(2)}, u32[]{:S(2)}) %collective-permute-start.1) | collective-permute-done | bytes 131104 | tf_op jit(solution)/shard_map/ppermute | solution.py:15
  55.7 140.9 %reduce-scatter.7.cloned.1.call-done = f32[8,4096]{1,0:T(8,128)} async-done(((f32[512,4096]{1,0:T(8,128)}), f32[8,4096]{1,0:T(8,128)}) %reduce-scatter.7.cloned.1.call-update) | async-done | bytes 131088 | tf_op jit(solution)/shard_map/reduce_scatter | solution.py:79
  196.6 1.0 multiply_reduce_fusion.1
  197.6 1.6 fusion
  199.3 0.4 convolution_bitcast_fusion.1
  199.8 0.4 convolution_multiply_fusion
  200.3 0.6 collective-permute-start.2
  200.9 246.5 %psum.14 = f32[4096]{0:T(1024)} all-reduce(f32[4096]{0:T(1024)S(1)} %get-tuple-element.10), channel_id=1, replica_groups=mesh['dp'=64,'tensor'=4] {'dp'}, use_global_device_ids=true, to_apply=%region_3.4 | all-reduce | flops 4096 | bytes 32768 | tf_op jit(solution)/shard_map/psum | solution.py:87
  447.4 2.7 collective-permute-start.3
  450.1 8.7 %fusion.33 = f32[512,768]{1,0:T(8,128)} fusion(bf16[512,4096]{1,0:T(8,128)(2,1)} %all-gather.2.cloned.1.call-done, f32[768]{0:T(1024)S(1)} %copy-done.2, bf16[4096,768]{1,0:T(8,128)(2,1)} %param.7), kind=kOutput, calls=%fused_computation.51 | convolution fusion | flops 3233808384 | bytes 12061696 | tf_op jit(solution)/shard_map/dot_general | solution.py:63
  458.9 0.7 select_convert_fusion
  459.5 12.4 %multiply_reduce_fusion = (f32[768]{0:T(1024)S(1)}, bf16[4096,768]{1,0:T(8,128)(2,1)}) fusion(f32[768]{0:T(1024)S(1)} %copy-done.2, bf16[4096,768]{1,0:T(8,128)(2,1)} %param.7, bf16[512,4096]{1,0:T(8,128)(2,1)} %all-gather.2.cloned.1.call-done, bf16[512,768]{1,0:T(8,128)(2,1)S(1)} %bitcast.26), kind=kOutput, calls=%fused_computation | convolution fusion | flops 3252681984 | bytes 17569792 | tf_op jit(solution)/shard_map/dot_general | solution.py:71
  472.0 10.3 %psum.15 = f32[768]{0:T(1024)} all-reduce(f32[768]{0:T(1024)S(1)} %get-tuple-element.12), channel_id=1, replica_groups=mesh['dp'=64,'tensor'=4] {'tensor'}, use_global_device_ids=true, to_apply=%region_5.6 | all-reduce | flops 768 | bytes 6144 | tf_op jit(solution)/shard_map/psum | solution.py:77
  482.3 1.7 convert_element_type.35
  (21 shorter events, 0.7 us)
Async XLA Ops:
  7.2 189.4 %reduce-scatter.7.cloned.1.call-start = ((), (), s32[]{:S(2)}) async-start(), calls=%async_computation.5 | async-start | bytes 8519680 | tf_op jit(solution)/shard_map/reduce_scatter | solution.py:79
  42.2 0.8 copy-start
  42.2 154.4 %copy-start.1 = (f32[4096]{0:T(1024)S(1)}, f32[4096]{0:T(1024)}, u32[]{:S(2)}) copy-start(f32[4096]{0:T(1024)} %param.6) | copy-start | bytes 49156
  42.2 408.0 %copy-start.2 = (f32[768]{0:T(1024)S(1)}, f32[768]{0:T(1024)}, u32[]{:S(2)}) copy-start(f32[768]{0:T(1024)} %param.8) | copy-start | bytes 9220
  42.2 407.9 %all-gather.2.cloned.1.call-start = ((), (), s32[]{:S(2)}) async-start(), calls=%async_computation.3 | async-start | bytes 4259840 | tf_op jit(solution)/shard_map/all_gather | solution.py:57
  44.0 5.1 %collective-permute-start = (f32[8,4096]{1,0:T(8,128)S(1)}, f32[8,4096]{1,0:T(8,128)S(1)}, u32[]{:S(2)}, u32[]{:S(2)}) collective-permute-start(f32[8,4096]{1,0:T(8,128)S(1)} %mul.67), channel_id=1, source_target_pairs={{0,1},{1,0},{2,3},{3,2},{4,5},{5,4},{6,7},{7,6},{8,9},{9,8},{10,11... | collective-permute-start | bytes 393224 | tf_op jit(solution)/shard_map/ppermute | solution.py:15
  49.1 6.6 %collective-permute-start.1 = (f32[8,4096]{1,0:T(8,128)S(1)}, f32[8,4096]{1,0:T(8,128)S(1)}, u32[]{:S(2)}, u32[]{:S(2)}) collective-permute-start(f32[8,4096]{1,0:T(8,128)S(1)} %add_select_fusion.1), channel_id=1, source_target_pairs={{0,2},{2,0},{1,3},{3,1},{4,6},{6,4},{5,7},{7,5},{8,10},{10,8},{9,1... | collective-permute-start | bytes 393224 | tf_op jit(solution)/shard_map/ppermute | solution.py:15
  199.2 283.1 %reduce-scatter.5.cloned.1.call-start = ((), (), s32[]{:S(2)}) async-start(), calls=%async_computation.4 | async-start | bytes 1966080 | tf_op jit(solution)/shard_map/reduce_scatter | solution.py:62
  200.3 247.1 %collective-permute-start.2 = (f32[8,4096]{1,0:T(8,128)S(1)}, f32[8,4096]{1,0:T(8,128)S(1)}, u32[]{:S(2)}, u32[]{:S(2)}) collective-permute-start(f32[8,4096]{1,0:T(8,128)S(1)} %mul.74), channel_id=1, source_target_pairs={{0,1},{1,0},{2,3},{3,2},{4,5},{5,4},{6,7},{7,6},{8,9},{9,8},{10,11... | collective-permute-start | bytes 393224 | tf_op jit(solution)/shard_map/ppermute | solution.py:15
  447.4 11.4 %collective-permute-start.3 = (f32[8,4096]{1,0:T(8,128)S(1)}, f32[8,4096]{1,0:T(8,128)S(1)}, u32[]{:S(2)}, u32[]{:S(2)}) collective-permute-start(f32[8,4096]{1,0:T(8,128)S(1)} %add_select_fusion), channel_id=1, source_target_pairs={{0,2},{2,0},{1,3},{3,1},{4,6},{6,4},{5,7},{7,5},{8,10},{10,8},{9,1... | collective-permute-start | bytes 393224 | tf_op jit(solution)/shard_map/ppermute | solution.py:15
Sparse Core Ops, SparseCore 0:
  42.3 154.2 reduce-scatter.6
  199.9 77.4 all-gather.1
  459.0 19.8 reduce-scatter.4
